TPU v7x, 256 devices: a whole 4x4x8 slice. The times are simulated.
256 devices in a mesh: dp: 4 (over y), expert: 64 (over x, z, core).
Axes of the slice: x: 4, y: 4, z: 8, core: 2. Of those that a mesh axis runs over, the one named last changes fastest.
Arguments:
- hidden: bfloat16 [32768, 2, 1024], P(('dp', 'expert')), may hold values from -6 to 6
- routes: int32 [32768, 2], P(('dp', 'expert')), may hold values from 0 to 63, all different within a row; in each aligned block of 128 rows (0 to 127, 128 to 255, ...) at most 8 rows name the same one
- gates: float32 [32768, 2], P(('dp', 'expert')), may hold values from 0.1 to 1
- cotangent: bfloat16 [32768, 7168], P(('dp', 'expert')), may hold values from -1.796875 to 1.796875
- weight: bfloat16 [64, 1024, 7168], P('expert', None, 'dp'), may hold values from -0.0625 to 0.0625
Outputs:
- grad_hidden: bfloat16 [32768, 2, 1024], P(('dp', 'expert'))
- grad_gates: float32 [32768, 2], P(('dp', 'expert'))
- grad_weight: bfloat16 [64, 1024, 7168], P('expert', None, 'dp')
Inputs may be any that keep to these rules, and one draw needn't show every extreme that they name: `routes`: each row names 2 different experts; in each aligned block of 128 rows (the rows of one device) no expert is named by more than 8 rows, a bound that some block reaches.
All inputs are finite; a program needn't handle non-finite values.
Results may differ from a plain program's by a relative error of at most 0.0049.
Values may be sent and summed in bfloat16 or wider, within the bound.
No kernel may reach another device: no remote copies, remote signals or barrier semaphores. Data moves between devices by JAX's collectives and lax.ppermute only.
A program may use at most 128 MiB of HBM per device.

v0:
```python
import jax
import jax.numpy as jnp
from jax import lax
from jax.sharding import PartitionSpec as P


def per_device(hidden, routes, gates, cotangent, weight):
    local_tokens, top_count, hidden_width = hidden.shape
    columns = lax.axis_size("expert")
    capacity = min(local_tokens, 2 * local_tokens * top_count // columns)
    slot_count = local_tokens * top_count
    flat_experts = routes.reshape(slot_count)
    one_hot = (flat_experts[:, None] == jnp.arange(columns, dtype=jnp.int32)[None, :]).astype(
        jnp.int32
    )
    earlier = jnp.cumsum(one_hot, axis=0) - one_hot
    position = jnp.sum(earlier * one_hot, axis=1)
    destination = flat_experts * capacity + position
    slot_of = (
        jnp.full((columns * capacity,), slot_count, jnp.int32)
        .at[destination]
        .set(jnp.arange(slot_count, dtype=jnp.int32))
    )
    scaled = (
        (gates[:, :, None] * hidden.astype(jnp.float32))
        .astype(jnp.bfloat16)
        .reshape(slot_count, hidden_width)
    )
    scaled = jnp.concatenate([scaled, jnp.zeros((1, hidden_width), jnp.bfloat16)], axis=0)
    cot_pad = jnp.concatenate([cotangent, jnp.zeros((1, cotangent.shape[1]), jnp.bfloat16)], axis=0)
    send_rows = scaled[slot_of].reshape(columns, capacity, hidden_width)
    send_cot = cot_pad[slot_of // top_count].reshape(columns, capacity, cotangent.shape[1])
    got_rows, got_cot = (
        lax.all_to_all(send_rows, "expert", split_axis=0, concat_axis=0, tiled=True),
        lax.all_to_all(send_cot, "expert", split_axis=0, concat_axis=0, tiled=True),
    )
    cot_quarter = lax.all_to_all(got_cot[None], "dp", split_axis=3, concat_axis=0, tiled=True)
    rows_all = lax.all_gather(got_rows[None], "dp", axis=0, tiled=True)
    matrix = weight[0]
    partial_back = jnp.einsum(
        "bscd,fd->bscf", cot_quarter, matrix, preferred_element_type=jnp.float32
    )
    summed = lax.psum_scatter(partial_back, "dp", scatter_dimension=0, tiled=True)
    grad_matrix = jnp.einsum(
        "bscf,bscd->fd", rows_all, cot_quarter, preferred_element_type=jnp.float32
    )
    returned = lax.all_to_all(summed[0], "expert", split_axis=0, concat_axis=0, tiled=True)
    back = returned.reshape(columns * capacity, hidden_width)[destination]
    grad_hidden = (
        (gates.reshape(slot_count)[:, None] * back)
        .astype(jnp.bfloat16)
        .reshape(local_tokens, top_count, hidden_width)
    )
    grad_gates = jnp.sum(
        hidden.reshape(slot_count, hidden_width).astype(jnp.float32) * back, axis=1
    ).reshape(local_tokens, top_count)
    return (grad_hidden, grad_gates, grad_matrix.astype(jnp.bfloat16)[None])


def solution(mesh):
    placed = (
        P(("dp", "expert"), None, None),
        P(("dp", "expert"), None),
        P(("dp", "expert"), None),
        P(("dp", "expert"), None),
        P("expert", None, "dp"),
    )
    return jax.shard_map(
        per_device,
        mesh=mesh,
        in_specs=placed,
        out_specs=(
            P(("dp", "expert"), None, None),
            P(("dp", "expert"), None),
            P("expert", None, "dp"),
        ),
        check_vma=False,
    )
```

profile of v0, /device:TPU:1, one launch (start us, length us, event | category | flops | bytes accessed | tf_op | source)
XLA Modules:
  0.0 613.7 jit_solution(7053803963562707793)
XLA Ops:
  7.2 0.0 reduce-scatter.2.cloned.1.call-start
  7.2 0.8 copy.29
  8.0 0.1 eq.29
  8.1 0.1 eq.25
  8.3 0.7 broadcast_multiply_fusion
  9.0 0.6 reduce-window.6
  9.6 0.2 slice_reduce_fusion
  9.8 0.1 copy.28
  9.9 0.1 mul.41
  10.1 0.1 fusion.14
  10.2 1.4 scatter_custom_fusion
  11.6 1.7 concatenate.6
  13.3 7.1 %gather_fusion = bf16[512,7168]{1,0:T(8,128)(2,1)} fusion(bf16[129,7168]{1,0:T(8,128)(2,1)S(1)} %concatenate.6, s32[1024]{0:T(1024)S(1)} %get-tuple-element.15), kind=kCustom, calls=%fused_computation | custom fusion | bytes 14682112 | tf_op jit(solution)/shard_map/gather | solution.py:32
  20.4 176.4 %all_to_all.33 = bf16[64,8,7168]{2,1,0:T(8,128)(2,1)} all-to-all(bf16[64,8,7168]{2,1,0:T(8,128)(2,1)} %bitcast.60), channel_id=1, replica_groups=mesh['dp'=4,'expert'=64] {'expert'}, dimensions={0} | all-to-all | bytes 14680064 | tf_op jit(solution)/shard_map/all_to_all | solution.py:35
  196.8 19.3 %copy.32 = bf16[1,64,8,7168]{1,2,0,3:T(8,128)(2,1)} copy(bf16[1,64,8,7168]{3,2,1,0:T(8,128)(2,1)} %bitcast.61) | data formatting | bytes 14680064 | tf_op jit(solution)/shard_map/broadcast_in_dim | solution.py:37
  216.1 14.8 %reshape.123 = bf16[4,2,458752]{2,1,0:T(2,128)(2,1)} reshape(bf16[7168,1,8,64]{3,2,1,0:T(8,128)(2,1)} %bitcast.57) | data formatting | bytes 14680064
  230.9 90.1 %all_to_all.34 = bf16[4,2,458752]{2,1,0:T(2,128)(2,1)} all-to-all(bf16[4,2,458752]{2,1,0:T(2,128)(2,1)} %reshape.123), channel_id=1, replica_groups=mesh['dp'=4,'expert'=64] {'dp'}, dimensions={0} | all-to-all | bytes 14680064 | tf_op jit(solution)/shard_map/all_to_all | solution.py:37
  321.0 14.3 %reshape.124 = bf16[7168,1,8,64]{3,2,1,0:T(8,128)(2,1)} reshape(bf16[4,2,458752]{2,1,0:T(2,128)(2,1)} %all_to_all.34) | data formatting | bytes 14680064
  335.3 17.7 %copy.34 = bf16[1,64,8,4,1792]{4,2,1,3,0:T(8,128)(2,1)} copy(bf16[1,64,8,4,1792]{1,2,4,3,0:T(8,128)(2,1)} %bitcast.58) | data formatting | bytes 14680064 | tf_op jit(solution)/shard_map/all_to_all | solution.py:37
  353.1 13.2 %fusion.2 = f32[4,64,8,1024]{3,2,1,0:T(8,128)} fusion(bf16[1,64,8,4,1792]{4,2,1,3,0:T(8,128)(2,1)} %copy.34, bf16[1,1024,1792]{2,1,0:T(8,128)(2,1)} %param.9), kind=kOutput, calls=%fused_computation.7 | convolution fusion | flops 7516192768 | bytes 19398656 | tf_op jit(solution)/shard_map/bscd,fd->bscf/dot_general | solution.py:40
  366.2 0.0 copy-start
  366.3 0.0 reduce-scatter.2.cloned.1.call-update
  366.3 78.2 %reduce-scatter.2.cloned.1.call-done = f32[1,64,8,1024]{3,2,1,0:T(8,128)} async-done(((f32[4,64,8,1024]{3,2,1,0:T(8,128)}), f32[1,64,8,1024]{3,2,1,0:T(8,128)}) %reduce-scatter.2.cloned.1.call-update) | async-done | bytes 2097168 | tf_op jit(solution)/shard_map/reduce_scatter | solution.py:43
  444.5 10.7 %all-to-all-start.2 = ((f32[64,8,1024]{2,1,0:T(8,128)}), f32[64,8,1024]{2,1,0:T(8,128)S(1)}, u32[]{:S(2)}, u32[]{:S(2)}) async-start(f32[64,8,1024]{2,1,0:T(8,128)} %bitcast.63), calls=%async_computation.3 | async-start | bytes 4194304 | tf_op jit(solution)/shard_map/all_to_all | solution.py:47
  455.2 0.0 all-gather.3.cloned.1.call-start
  455.3 0.0 copy-done
  455.3 0.1 copy.27
  455.4 51.0 %all-to-all-done.2 = f32[64,8,1024]{2,1,0:T(8,128)S(1)} async-done(((f32[64,8,1024]{2,1,0:T(8,128)}), f32[64,8,1024]{2,1,0:T(8,128)S(1)}, u32[]{:S(2)}, u32[]{:S(2)}) %all-to-all-start.2) | async-done | bytes 2097184 | tf_op jit(solution)/shard_map/all_to_all | solution.py:47
  506.4 1.1 gather_fusion.1
  507.5 0.6 gather.13
  508.1 3.0 fusion.10
  511.2 0.2 reshape.81
  511.4 2.1 gather_fusion.2
  513.5 34.3 %all_to_all.35 = bf16[64,8,1024]{2,1,0:T(8,128)(2,1)} all-to-all(bf16[64,8,1024]{2,1,0:T(8,128)(2,1)S(1)} %bitcast.62), channel_id=1, replica_groups=mesh['dp'=4,'expert'=64] {'expert'}, dimensions={0} | all-to-all | bytes 2097152 | tf_op jit(solution)/shard_map/all_to_all | solution.py:34
  547.7 0.0 all-gather.3.cloned.1.call-update
  547.8 0.6 copy.35
  548.4 45.4 %all-gather.3.cloned.1.call-done = bf16[256,8,1024]{2,1,0:T(8,128)(2,1)} async-done(((bf16[64,8,1024]{2,1,0:T(8,128)(2,1)}), bf16[256,8,1024]{2,1,0:T(8,128)(2,1)}) %all-gather.3.cloned.1.call-update) | async-done | bytes 4194320 | tf_op jit(solution)/shard_map/all_gather | solution.py:38
  593.8 13.0 %fusion.7 = bf16[1,1024,1792]{2,1,0:T(8,128)(2,1)} fusion(bf16[4,64,8,1024]{3,2,1,0:T(8,128)(2,1)} %bitcast.67, bf16[1,64,8,4,1792]{4,2,1,3,0:T(8,128)(2,1)} %copy.34), kind=kOutput, calls=%fused_computation.10 | convolution fusion | flops 7518027776 | bytes 15204352 | tf_op jit(solution)/shard_map/bscf,bscd->fd/dot_general | solution.py:44
  (9 shorter events, 0.1 us)
Async XLA Ops:
  7.2 437.3 %reduce-scatter.2.cloned.1.call-start = ((), (), s32[]{:S(2)}) async-start(), calls=%async_computation.5 | async-start | bytes 10485760 | tf_op jit(solution)/shard_map/reduce_scatter | solution.py:43
  366.2 89.0 %copy-start = (f32[128,2]{0,1:T(2,128)S(1)}, f32[128,2]{0,1:T(2,128)}, u32[]{:S(2)}) copy-start(f32[128,2]{0,1:T(2,128)} %param.7) | copy-start | bytes 3076
  444.5 61.9 %all-to-all-start.2 = ((f32[64,8,1024]{2,1,0:T(8,128)}), f32[64,8,1024]{2,1,0:T(8,128)S(1)}, u32[]{:S(2)}, u32[]{:S(2)}) async-start(f32[64,8,1024]{2,1,0:T(8,128)} %bitcast.63), calls=%async_computation.3 | async-start | bytes 4194304 | tf_op jit(solution)/shard_map/all_to_all | solution.py:47
  455.2 138.6 %all-gather.3.cloned.1.call-start = ((), (), s32[]{:S(2)}) async-start(), calls=%async_computation.6 | async-start | bytes 5242880 | tf_op jit(solution)/shard_map/all_gather | solution.py:38
Sparse Core Ops, SparseCore 0:
  366.4 78.0 reduce-scatter.1
  547.9 45.8 all-gather.2
where the time goes:
time: 615 us; the launch traced here: 614 us
  blocking collectives  301 us (49%)
  waiting for transfers between devices  175 us (28%)
  local copies, waits for them, and re-layouts  82.5 us (13%)
  matrix products  26.2 us (4%)
  between operations  14.2 us (2%)
  starting transfers between devices  10.8 us (2%)
    all_to_all x1, blocking collectives, per_device(): lax.all_to_all(send_cot, 'expert', split_axis=0, concat_axis=0, tiled=True)  176 us
    all_to_all x1, blocking collectives, per_device(): lax.all_to_all(got_cot[None], 'dp', split_axis=3, concat_axis=0, tiled=True)  90.1 us
    reduce_scatter x1, waiting for transfers between devices, per_device(): lax.psum_scatter(partial_back, 'dp', scatter_dimension=0, tiled=True)  78.2 us
    all_to_all x1, waiting for transfers between devices, per_device(): lax.all_to_all(summed[0], 'expert', split_axis=0, concat_axis=0, tiled=True)  51 us
    all_gather x1, waiting for transfers between devices, per_device(): rows_all = lax.all_gather(got_rows[None], 'dp', axis=0, tiled=True)  45.4 us
    all_to_all x1, blocking collectives, per_device(): lax.all_to_all(send_rows, 'expert', split_axis=0, concat_axis=0, tiled=True)  34.3 us
    unnamed x7, local copies, waits for them, and re-layouts  30.6 us
    broadcast_in_dim x1, local copies, waits for them, and re-layouts, per_device(): got_cot[None]  19.3 us
  transfers between devices with their start and end apart: 3, of which 3 were waited for; matrix products, arithmetic and copies ran while one was open for 0% of the time, Pallas kernels for 0%

commit v1 on v0

--- a/solution.py
+++ b/solution.py
@@ -34,7 +34,12 @@
         lax.all_to_all(send_rows, "expert", split_axis=0, concat_axis=0, tiled=True),
         lax.all_to_all(send_cot, "expert", split_axis=0, concat_axis=0, tiled=True),
     )
-    cot_quarter = lax.all_to_all(got_cot[None], "dp", split_axis=3, concat_axis=0, tiled=True)
+    cot_quarter = jnp.concatenate(
+        lax.all_to_all(
+            jnp.stack(jnp.split(got_cot[None], lax.axis_size("dp"), axis=3)), "dp", 0, 0
+        ),
+        axis=0,
+    )
     rows_all = lax.all_gather(got_rows[None], "dp", axis=0, tiled=True)
     matrix = weight[0]
     partial_back = jnp.einsum(

time: 615 us -> 546 us (0.89)
  local copies, waits for them, and re-layouts: 82.5 us -> 19.9 us
    unnamed x7 -> x9, local copies, waits for them, and re-layouts: 30.6 us -> 4.55 us
    broadcast_in_dim x1 -> x0, local copies, waits for them, and re-layouts: 19.3 us -> none  [per_device(): got_cot[None]]
    all_to_all x1 -> x0, local copies, waits for them, and re-layouts: 17.7 us -> none  [per_device(): lax.all_to_all(got_cot[None], 'dp', split_axis=3, concat_axis=0, tiled=True)]
where the time goes in v1:
time: 546 us
  blocking collectives  297 us (54%)
  waiting for transfers between devices  175 us (32%)
  matrix products  23 us (4%)
  local copies, waits for them, and re-layouts  19.9 us (4%)
  between operations  14.2 us (3%)
  starting transfers between devices  11 us (2%)
  other arithmetic  5.51 us (1%)
    all_to_all x1, blocking collectives, per_device(): lax.all_to_all(send_cot, 'expert', split_axis=0, concat_axis=0, tiled=True)  176 us
    all_to_all x1, blocking collectives, per_device(): lax.all_to_all(jnp.stack(jnp.split(got_cot[None], lax.axis_size('dp'), ax...  86.6 us
    reduce_scatter x1, waiting for transfers between devices, per_device(): lax.psum_scatter(partial_back, 'dp', scatter_dimension=0, tiled=True)  78.7 us
    all_to_all x1, waiting for transfers between devices, per_device(): lax.all_to_all(summed[0], 'expert', split_axis=0, concat_axis=0, tiled=True)  50.8 us
    all_gather x1, waiting for transfers between devices, per_device(): rows_all = lax.all_gather(got_rows[None], 'dp', axis=0, tiled=True)  45.4 us
    all_to_all x1, blocking collectives, per_device(): lax.all_to_all(send_rows, 'expert', split_axis=0, concat_axis=0, tiled=True)  34.3 us
    dot_general x1, matrix products, per_device(): jnp.einsum('bscf,bscd->fd', rows_all, cot_quarter, preferred_element_type...  13 us
  transfers between devices with their start and end apart: 3, of which 3 were waited for; matrix products, arithmetic and copies ran while one was open for 0% of the time, Pallas kernels for 0%

profile of v1, /device:TPU:1, one launch (start us, length us, event | category | flops | bytes accessed | tf_op | source)
XLA Modules:
  0.0 545.7 jit_solution(17191187257097761906)
XLA Ops:
  7.2 0.0 reduce-scatter.2.cloned.1.call-start
  7.2 0.8 copy.25
  8.0 0.1 eq.29
  8.1 0.1 eq.25
  8.3 0.7 broadcast_multiply_fusion
  9.0 0.6 reduce-window.6
  9.6 0.2 slice_reduce_fusion
  9.8 0.1 copy.24
  9.9 0.1 mul.41
  10.1 0.1 fusion.14
  10.2 1.4 scatter_custom_fusion
  11.6 1.7 concatenate.6
  13.3 7.1 %gather_fusion = bf16[512,7168]{1,0:T(8,128)(2,1)} fusion(bf16[129,7168]{1,0:T(8,128)(2,1)S(1)} %concatenate.6, s32[1024]{0:T(1024)S(1)} %get-tuple-element.16), kind=kCustom, calls=%fused_computation | custom fusion | bytes 14682112 | tf_op jit(solution)/shard_map/gather | solution.py:32
  20.4 176.3 %all_to_all.20 = bf16[64,8,7168]{2,1,0:T(8,128)(2,1)S(1)} all-to-all(bf16[64,8,7168]{2,1,0:T(8,128)(2,1)} %bitcast.61), channel_id=1, replica_groups=mesh['dp'=4,'expert'=64] {'expert'}, dimensions={0} | all-to-all | bytes 14680064 | tf_op jit(solution)/shard_map/all_to_all | solution.py:35
  196.7 0.5 slice_bitcast_fusion.3
  197.2 1.0 pad_maximum_fusion
  198.2 0.0 copy-start.2
  198.2 86.6 %all_to_all.21 = bf16[4,1,64,8,1792]{4,3,2,1,0:T(8,128)(2,1)S(1)} all-to-all(bf16[4,1,64,8,1792]{4,3,2,1,0:T(8,128)(2,1)S(1)} %pad_maximum_fusion), channel_id=1, replica_groups=mesh['dp'=4,'expert'=64] {'dp'}, dimensions={0} | all-to-all | bytes 14680064 | tf_op jit(solution)/shard_map/all_to_all | solution.py:38
  284.8 0.0 copy-start
  284.8 3.0 copy-done
  287.8 0.0 copy-done.2
  287.8 10.0 %fusion.2 = f32[4,64,8,1024]{3,2,1,0:T(8,128)} fusion(bf16[4,1,64,8,1792]{4,3,2,1,0:T(8,128)(2,1)S(1)} %all_to_all.21, bf16[1,1024,1792]{2,1,0:T(8,128)(2,1)S(1)} %copy-done.2), kind=kOutput, calls=%fused_computation.8 | convolution fusion | flops 7516192768 | bytes 19398656 | tf_op jit(solution)/shard_map/bscd,fd->bscf/dot_general | solution.py:45
  297.8 0.0 reduce-scatter.2.cloned.1.call-update
  297.8 0.0 copy-start.1
  297.8 78.7 %reduce-scatter.2.cloned.1.call-done = f32[1,64,8,1024]{3,2,1,0:T(8,128)} async-done(((f32[4,64,8,1024]{3,2,1,0:T(8,128)}), f32[1,64,8,1024]{3,2,1,0:T(8,128)}) %reduce-scatter.2.cloned.1.call-update) | async-done | bytes 2097168 | tf_op jit(solution)/shard_map/reduce_scatter | solution.py:48
  376.5 10.7 %all-to-all-start.2 = ((f32[64,8,1024]{2,1,0:T(8,128)}), f32[64,8,1024]{2,1,0:T(8,128)S(1)}, u32[]{:S(2)}, u32[]{:S(2)}) async-start(f32[64,8,1024]{2,1,0:T(8,128)} %bitcast.64), calls=%async_computation.3 | async-start | bytes 4194304 | tf_op jit(solution)/shard_map/all_to_all | solution.py:52
  387.2 0.2 all-gather.3.cloned.1.call-start
  387.5 0.0 copy-done.1
  387.5 0.1 copy.23
  387.6 50.8 %all-to-all-done.2 = f32[64,8,1024]{2,1,0:T(8,128)S(1)} async-done(((f32[64,8,1024]{2,1,0:T(8,128)}), f32[64,8,1024]{2,1,0:T(8,128)S(1)}, u32[]{:S(2)}, u32[]{:S(2)}) %all-to-all-start.2) | async-done | bytes 2097184 | tf_op jit(solution)/shard_map/all_to_all | solution.py:52
  438.4 1.1 gather_fusion.1
  439.5 0.6 gather.13
  440.1 3.0 fusion.10
  443.2 0.2 reshape.85
  443.4 2.1 gather_fusion.2
  445.5 34.3 %all_to_all.22 = bf16[64,8,1024]{2,1,0:T(8,128)(2,1)} all-to-all(bf16[64,8,1024]{2,1,0:T(8,128)(2,1)S(1)} %bitcast.63), channel_id=1, replica_groups=mesh['dp'=4,'expert'=64] {'expert'}, dimensions={0} | all-to-all | bytes 2097152 | tf_op jit(solution)/shard_map/all_to_all | solution.py:34
  479.8 0.0 all-gather.3.cloned.1.call-update
  479.8 0.6 copy.28
  480.4 45.4 %all-gather.3.cloned.1.call-done = bf16[256,8,1024]{2,1,0:T(8,128)(2,1)} async-done(((bf16[64,8,1024]{2,1,0:T(8,128)(2,1)}), bf16[256,8,1024]{2,1,0:T(8,128)(2,1)}) %all-gather.3.cloned.1.call-update) | async-done | bytes 4194320 | tf_op jit(solution)/shard_map/all_gather | solution.py:43
  525.8 13.0 %fusion.7 = bf16[1,1024,1792]{2,1,0:T(8,128)(2,1)} fusion(bf16[4,64,8,1024]{3,2,1,0:T(8,128)(2,1)} %bitcast.68, bf16[4,1,64,8,1792]{4,3,2,1,0:T(8,128)(2,1)} %copy-done), kind=kOutput, calls=%fused_computation.11 | convolution fusion | flops 7518027776 | bytes 15204352 | tf_op jit(solution)/shard_map/bscf,bscd->fd/dot_general | solution.py:49
  (9 shorter events, 0.1 us)
Async XLA Ops:
  7.2 369.3 %reduce-scatter.2.cloned.1.call-start = ((), (), s32[]{:S(2)}) async-start(), calls=%async_computation.5 | async-start | bytes 10485760 | tf_op jit(solution)/shard_map/reduce_scatter | solution.py:48
  198.2 89.6 %copy-start.2 = (bf16[1,1024,1792]{2,1,0:T(8,128)(2,1)S(1)}, bf16[1,1024,1792]{2,1,0:T(8,128)(2,1)}, u32[]{:S(2)}) copy-start(bf16[1,1024,1792]{2,1,0:T(8,128)(2,1)} %param.9) | copy-start | bytes 11010052
  284.8 3.0 copy-start
  297.8 89.7 %copy-start.1 = (f32[128,2]{0,1:T(2,128)S(1)}, f32[128,2]{0,1:T(2,128)}, u32[]{:S(2)}) copy-start(f32[128,2]{0,1:T(2,128)} %param.7) | copy-start | bytes 3076
  376.5 61.9 %all-to-all-start.2 = ((f32[64,8,1024]{2,1,0:T(8,128)}), f32[64,8,1024]{2,1,0:T(8,128)S(1)}, u32[]{:S(2)}, u32[]{:S(2)}) async-start(f32[64,8,1024]{2,1,0:T(8,128)} %bitcast.64), calls=%async_computation.3 | async-start | bytes 4194304 | tf_op jit(solution)/shard_map/all_to_all | solution.py:52
  387.2 138.6 %all-gather.3.cloned.1.call-start = ((), (), s32[]{:S(2)}) async-start(), calls=%async_computation.6 | async-start | bytes 5242880 | tf_op jit(solution)/shard_map/all_gather | solution.py:43
Sparse Core Ops, SparseCore 0:
  297.9 78.5 reduce-scatter.1
  479.9 45.8 all-gather.2
